TPU v7x, 256 devices: a whole 4x4x8 slice. The times are simulated.
256 devices in a mesh: blk: 32 (over z, y_lo, core), grp: 8 (over x, y_hi).
Axes of the slice: x: 4, y: 4 (y_hi: 2, y_lo: 2; y = y_hi * 2 + y_lo), z: 8, core: 2. Of those that a mesh axis runs over, the one named last changes fastest.
Arguments:
- low_sites: float32 [8, 32768], P(None, ('blk', 'grp')), may hold values from -6 to 6
- low_probes: float32 [8, 32768], P(None, ('blk', 'grp')), may hold values from -0.03314563 to 0.03314563
- high_probes: float32 [8, 16384], P(None, ('blk', 'grp')), may hold values from -0.03314563 to 0.03314563
- nested: int32 [16384], P(('blk', 'grp')), may hold values from 0 to 32767, as said below
- inv_len_low: float32 [8], replicated, may hold values from 0.15 to 0.6
- inv_len_diff: float32 [8], replicated, may hold values from 0.2 to 0.8
Outputs:
- low_out: float32 [8, 32768], P(None, ('blk', 'grp'))
- high_out: float32 [8, 16384], P(None, ('blk', 'grp'))
Inputs may be any that keep to these rules, and one draw needn't show every extreme that they name: `nested`: entries are distinct; the high sites in the aligned block of 512 entries number b all lie among the low sites b * 1024 to (b + 1) * 1024 - 1.
All inputs are finite; a program needn't handle non-finite values.
Results may differ from a plain program's by a relative error of at most 0.00021.
Values sent between devices are 32-bit elements; how exact they have to be, the bound alone decides.
No kernel may reach another device: no remote copies, remote signals or barrier semaphores. Data moves between devices by JAX's collectives and lax.ppermute only.
A program may use at most 64 MiB of HBM per device.

v0:
```python
import math

import jax
import jax.numpy as jnp
from jax import lax
from jax.sharding import PartitionSpec as P

RHO = 0.9
VAR_DIFF = 1.0
SQRT_THREE = 1.7320508075688772


def matern(rows, cols):
    inner = jnp.einsum("fr,fc->rc", rows, cols, precision=lax.Precision.HIGHEST)
    square = jnp.sum(rows * rows, 0)[:, None] + jnp.sum(cols * cols, 0)[None, :] - 2.0 * inner
    dist = jnp.sqrt(jnp.maximum(square, 0.0))
    return (1.0 + SQRT_THREE * dist) * jnp.exp(-SQRT_THREE * dist)


def partial_product(rows, cols, weights):
    tile = matern(rows, cols)
    return jnp.einsum("pc,rc->pr", weights, tile, precision=lax.Precision.HIGHEST)


def apply_blocked(rows, cols, weights):
    count = cols.shape[1]
    step = math.gcd(count, 2048)
    blocks = count // step
    cols_split = cols.reshape(cols.shape[0], blocks, step).transpose(1, 0, 2)
    weights_split = weights.reshape(weights.shape[0], blocks, step).transpose(1, 0, 2)

    def one_block(total, item):
        return (total + partial_product(rows, item[0], item[1]), None)

    start = jnp.zeros((weights.shape[0], rows.shape[1]), jnp.float32)
    total, _ = lax.scan(one_block, start, (cols_split, weights_split))
    return total


def per_device(low_sites, low_probes, high_probes, nested, inv_len_low, inv_len_diff):
    rows_dev = low_sites.shape[1]
    feats_block, lowp_block, highp_block = (
        lax.all_gather(low_sites, "grp", axis=1, tiled=True),
        lax.all_gather(low_probes, "grp", axis=1, tiled=True),
        lax.all_gather(high_probes, "grp", axis=1, tiled=True),
    )
    nest_block = lax.all_gather(nested, "grp", axis=0, tiled=True)
    width = feats_block.shape[1]
    base = lax.axis_index("blk") * width
    place_block = nest_block - base
    own_place = nested - base
    slots = lax.broadcasted_iota(jnp.int32, (width,), 0)
    pick_own = (slots[:, None] == own_place[None, :]).astype(jnp.float32)
    high_feats = jnp.dot(
        feats_block, pick_own, precision=lax.Precision.HIGHEST, preferred_element_type=jnp.float32
    )
    rows_low = low_sites * inv_len_low[:, None]
    rows_diff = high_feats * inv_len_diff[:, None]
    own_slots = lax.axis_index("grp") * rows_dev + lax.broadcasted_iota(jnp.int32, (rows_dev,), 0)
    spread_own = (place_block[:, None] == own_slots[None, :]).astype(jnp.float32)
    mixed_own = low_probes + RHO * jnp.dot(
        highp_block, spread_own, precision=lax.Precision.HIGHEST, preferred_element_type=jnp.float32
    )
    cols_feat = lax.all_gather(low_sites, ("blk", "grp"), axis=1, tiled=True)
    cols_weight = lax.all_gather(mixed_own, ("blk", "grp"), axis=1, tiled=True)
    cols_high = lax.all_gather(high_feats, ("blk", "grp"), axis=1, tiled=True)
    cols_hprobe = lax.all_gather(high_probes, ("blk", "grp"), axis=1, tiled=True)
    low_cols = cols_feat * inv_len_low[:, None]
    new_low = apply_blocked(rows_low, low_cols, cols_weight)
    new_diff = VAR_DIFF * apply_blocked(rows_diff, cols_high * inv_len_diff[:, None], cols_hprobe)
    low_block = lax.all_gather(new_low, "grp", axis=1, tiled=True)
    high_part = jnp.dot(
        low_block, pick_own, precision=lax.Precision.HIGHEST, preferred_element_type=jnp.float32
    )
    high_out = RHO * high_part + new_diff
    return (new_low, high_out)


def solution(mesh):
    return jax.shard_map(
        per_device,
        mesh=mesh,
        in_specs=(
            P(None, ("blk", "grp")),
            P(None, ("blk", "grp")),
            P(None, ("blk", "grp")),
            P(("blk", "grp")),
            P(),
            P(),
        ),
        out_specs=(P(None, ("blk", "grp")), P(None, ("blk", "grp"))),
        check_vma=False,
    )
```

profile of v0, /device:TPU:16, one launch (start us, length us, event | category | flops | bytes accessed | tf_op | source)
XLA Modules:
  0.0 1463.8 jit_solution(3234751607387825071)
XLA Ops:
  8.0 34.4 %all-gather = f32[8,64,8]{1,2,0:T(8,128)S(1)} all-gather(f32[1,64,8]{1,2,0:T(8,128)S(1)} %bitcast.97), channel_id=1, replica_groups=mesh['blk'=32,'grp'=8] {'grp'}, dimensions={0}, use_global_device_ids=true | all-gather | bytes 18432 | tf_op jit(solution)/shard_map/all_gather | solution.py:45
  45.2 13.1 all-reduce
  60.5 32.2 %all_gather.30 = f32[8,1024]{1,0:T(8,128)S(1)} all-gather(f32[8,128]{1,0:T(8,128)S(1)} %copy-done), channel_id=1, replica_groups=mesh['blk'=32,'grp'=8] {'grp'}, dimensions={1}, use_global_device_ids=true | all-gather | bytes 36864 | tf_op jit(solution)/shard_map/all_gather | solution.py:43
  92.7 627.3 %all-gather.1 = f32[256,64,8]{1,2,0:T(8,128)S(1)} all-gather(f32[1,64,8]{1,2,0:T(8,128)S(1)} %bitcast.98), channel_id=1, replica_groups=mesh['blk'=32,'grp'=8] {'blk','grp'}, dimensions={0}, use_global_device_ids=true | all-gather | bytes 526336 | tf_op jit(solution)/shard_map/all_gather | solution.py:67
  720.3 626.3 %all-gather.2 = f32[256,64,8]{1,2,0:T(8,128)S(1)} all-gather(f32[1,64,8]{1,2,0:T(8,128)S(1)} %bitcast.99), channel_id=1, replica_groups=mesh['blk'=32,'grp'=8] {'blk','grp'}, dimensions={0}, use_global_device_ids=true | all-gather | bytes 526336 | tf_op jit(solution)/shard_map/all_gather | solution.py:66
  1348.9 12.1 while.27
  1362.4 61.5 %while.26 = (s32[]{:T(128)}, f32[8,128]{1,0:T(8,128)S(1)}, f32[16,8,2048]{2,1,0:T(8,128)}, f32[128]{0:T(128)S(1)}, f32[16,8,2048]{2,1,0:T(8,128)S(1)}, /*index=5*/f32[8,128]{1,0:T(8,128)S(1)}, s32[]{:T(128)}, s32[]{:T(128)}) while((s32[]{:T(128)}, f32[8,128]{1,0:T(8,128)S(1)}, f32[16,8,2048]{2,1,0:T(8,128)}, f32[128]{0:T(128)S(1)}, ...), condition=%wide.region_3.4_spmd.clone, body=%wide.region_1.3_spmd.clone.sunk | while | flops 52461568 | bytes 2323059 | solution.py:36
  1362.4 2.1 fusion.65
  1366.3 2.1 fusion.65
  1370.1 2.1 fusion.65
  1372.2 1.7 convolution_add_fusion.4
  1373.9 2.1 fusion.65
  1376.1 1.7 convolution_add_fusion.4
  1377.8 2.1 fusion.65
  1381.6 2.1 fusion.65
  1385.5 2.1 fusion.65
  1387.6 1.7 convolution_add_fusion.4
  1389.3 2.1 fusion.65
  1391.5 1.7 convolution_add_fusion.4
  1393.2 2.1 fusion.65
  1397.0 2.1 fusion.65
  1399.1 1.7 convolution_add_fusion.4
  1400.8 2.1 fusion.65
  1403.0 1.7 convolution_add_fusion.4
  1404.7 2.1 fusion.65
  1406.8 1.7 convolution_add_fusion.4
  1408.5 2.1 fusion.65
  1412.4 2.1 fusion.65
  1414.5 1.7 convolution_add_fusion.4
  1416.2 2.1 fusion.65
  1420.1 2.1 fusion.65
  1423.9 32.2 %all_gather.28 = f32[8,1024]{1,0:T(8,128)S(1)} all-gather(f32[8,128]{1,0:T(8,128)S(1)} %get-tuple-element.132), channel_id=1, replica_groups=mesh['blk'=32,'grp'=8] {'grp'}, dimensions={1}, use_global_device_ids=true | all-gather | bytes 36864 | tf_op jit(solution)/shard_map/all_gather | solution.py:71
  (100 shorter events, 35.3 us)
Async XLA Ops:
  7.2 0.8 copy-start.1
  7.2 1353.8 %all-gather.8.cloned.1.call-start = ((), (), s32[]{:S(2)}) async-start(), calls=%async_computation.1 | async-start | bytes 1052672 | tf_op jit(solution)/shard_map/all_gather | solution.py:64
  7.9 1354.5 %all-gather.6.cloned.1.call-start = ((), (), s32[]{:S(2)}) async-start(), calls=%async_computation | async-start | bytes 1052672 | tf_op jit(solution)/shard_map/all_gather | solution.py:65
  42.4 0.7 copy-start.7
  44.3 0.7 copy-start.6
  58.3 0.7 copy-start.5
  59.9 0.7 copy-start
  92.7 627.3 %copy-start.4 = (f32[8]{0:T(128)S(1)}, f32[8]{0:T(128)}, u32[]{:S(2)}) copy-start(f32[8]{0:T(128)} %param.14) | copy-start | bytes 100
  1346.8 0.7 copy-start.3
  1423.9 32.2 %copy-start.2 = (f32[8,128]{1,0:T(8,128)}, f32[8,128]{1,0:T(8,128)S(1)}, u32[]{:S(2)}) copy-start(f32[8,128]{1,0:T(8,128)S(1)} %get-tuple-element.132) | copy-start | bytes 12292
Sparse Core Ops, SparseCore 0:
  9.8 539.7 all-gather.7
  551.9 541.4 all-gather.5
where the time goes:
time: 1470 us; the launch traced here: 1460 us
  blocking collectives  1370 us (93%)
  matrix products  73 us (5%)
  between operations  14.8 us (1%)
    all_gather x1, blocking collectives, per_device(): lax.all_gather(high_probes, ('blk', 'grp'), axis=1, tiled=True)  627 us
    all_gather x1, blocking collectives, per_device(): cols_high = lax.all_gather(high_feats, ('blk', 'grp'), axis=1, tiled=True)  626 us
    dot_general x24, matrix products, matern(): inner = jnp.einsum('fr,fc->rc', rows, cols, precision=lax.Precision.HIGHEST)  40.2 us
    all_gather x1, blocking collectives, per_device(): lax.all_gather(high_probes, 'grp', axis=1, tiled=True)  34.4 us
    all_gather x1, blocking collectives, per_device(): low_block = lax.all_gather(new_low, 'grp', axis=1, tiled=True)  32.2 us
    all_gather x1, blocking collectives, per_device(): lax.all_gather(low_sites, 'grp', axis=1, tiled=True)  32.2 us
    dot_general x24, matrix products, partial_product(): jnp.einsum('pc,rc->pr', weights, tile, precision=lax.Precision.HIGHEST)  30.7 us
  transfers between devices with their start and end apart: 2, of which 0 were waited for; matrix products, arithmetic and copies ran while one was open for 1% of the time, Pallas kernels for 0%

commit v1 on v0

--- a/solution.py
+++ b/solution.py
@@ -8,6 +8,9 @@
 RHO = 0.9
 VAR_DIFF = 1.0
 SQRT_THREE = 1.7320508075688772
+
+GRP_BITS = (2, 0, 1)
+BLK_BITS = (4, 3, 2, 1, 0)
 
 
 def matern(rows, cols):
@@ -37,38 +40,86 @@
     return total
 
 
+def gather_bits(x, axis, size, bits):
+    me = lax.axis_index(axis)
+    buf = x[None]
+    for bit in bits:
+        mask = 1 << bit
+        other = lax.ppermute(buf, axis, [(i, i ^ mask) for i in range(size)])
+        upper = ((me >> bit) & 1) == 1
+        low = jnp.where(upper, other, buf)
+        high = jnp.where(upper, buf, other)
+        buf = jnp.concatenate([low, high], 0)
+    k = len(bits)
+    buf = buf.reshape((2,) * k + x.shape)
+    order = sorted(range(k), key=lambda i: -bits[k - 1 - i])
+    buf = buf.transpose(tuple(order) + tuple(range(k, k + x.ndim)))
+    return buf.reshape((size,) + x.shape)
+
+
 def per_device(low_sites, low_probes, high_probes, nested, inv_len_low, inv_len_diff):
-    rows_dev = low_sites.shape[1]
-    feats_block, lowp_block, highp_block = (
-        lax.all_gather(low_sites, "grp", axis=1, tiled=True),
-        lax.all_gather(low_probes, "grp", axis=1, tiled=True),
-        lax.all_gather(high_probes, "grp", axis=1, tiled=True),
+    feats_n, rows_dev = low_sites.shape
+    probes_n = low_probes.shape[0]
+    highs_dev = high_probes.shape[1]
+    grp_size = 1 << len(GRP_BITS)
+    blk_size = 1 << len(BLK_BITS)
+
+    packet = jnp.concatenate(
+        [low_sites.reshape(-1), low_probes.reshape(-1), high_probes.reshape(-1), nested.astype(jnp.float32)]
     )
-    nest_block = lax.all_gather(nested, "grp", axis=0, tiled=True)
+    got = gather_bits(packet, "grp", grp_size, GRP_BITS)
+    cuts = [feats_n * rows_dev, probes_n * rows_dev, probes_n * highs_dev, highs_dev]
+    pieces = []
+    start = 0
+    for c in cuts:
+        pieces.append(got[:, start:start + c])
+        start += c
+
+    def unblock(piece, rows):
+        return piece.reshape(grp_size, rows, -1).transpose(1, 0, 2).reshape(rows, -1)
+
+    feats_block = unblock(pieces[0], feats_n)
+    lowp_block = unblock(pieces[1], probes_n)
+    highp_block = unblock(pieces[2], probes_n)
+    nest_block = pieces[3].reshape(-1).astype(jnp.int32)
+
     width = feats_block.shape[1]
     base = lax.axis_index("blk") * width
     place_block = nest_block - base
-    own_place = nested - base
     slots = lax.broadcasted_iota(jnp.int32, (width,), 0)
-    pick_own = (slots[:, None] == own_place[None, :]).astype(jnp.float32)
-    high_feats = jnp.dot(
-        feats_block, pick_own, precision=lax.Precision.HIGHEST, preferred_element_type=jnp.float32
+    pick = (slots[:, None] == place_block[None, :]).astype(jnp.float32)
+    high_feats_block = jnp.dot(
+        feats_block, pick, precision=lax.Precision.HIGHEST, preferred_element_type=jnp.float32
     )
+    spread = lax.dot_general(
+        highp_block, pick, (((1,), (1,)), ((), ())),
+        precision=lax.Precision.HIGHEST, preferred_element_type=jnp.float32,
+    )
+    mixed_block = lowp_block + RHO * spread
+
+    own_high = lax.axis_index("grp") * highs_dev
+    high_feats = lax.dynamic_slice_in_dim(high_feats_block, own_high, highs_dev, 1)
+    pick_own = lax.dynamic_slice_in_dim(pick, own_high, highs_dev, 1)
+
+    wide = jnp.concatenate([feats_block, mixed_block, high_feats_block, highp_block], 1)
+    every = gather_bits(wide, "blk", blk_size, BLK_BITS)
+    nb = width
+    nh = high_feats_block.shape[1]
+
+    def unstack(part):
+        return part.transpose(1, 0, 2).reshape(part.shape[1], -1)
+
+    cols_feat = unstack(every[:, :, :nb])
+    cols_weight = unstack(every[:, :, nb:2 * nb])
+    cols_high = unstack(every[:, :, 2 * nb:2 * nb + nh])
+    cols_hprobe = unstack(every[:, :, 2 * nb + nh:])
+
     rows_low = low_sites * inv_len_low[:, None]
     rows_diff = high_feats * inv_len_diff[:, None]
-    own_slots = lax.axis_index("grp") * rows_dev + lax.broadcasted_iota(jnp.int32, (rows_dev,), 0)
-    spread_own = (place_block[:, None] == own_slots[None, :]).astype(jnp.float32)
-    mixed_own = low_probes + RHO * jnp.dot(
-        highp_block, spread_own, precision=lax.Precision.HIGHEST, preferred_element_type=jnp.float32
-    )
-    cols_feat = lax.all_gather(low_sites, ("blk", "grp"), axis=1, tiled=True)
-    cols_weight = lax.all_gather(mixed_own, ("blk", "grp"), axis=1, tiled=True)
-    cols_high = lax.all_gather(high_feats, ("blk", "grp"), axis=1, tiled=True)
-    cols_hprobe = lax.all_gather(high_probes, ("blk", "grp"), axis=1, tiled=True)
     low_cols = cols_feat * inv_len_low[:, None]
     new_low = apply_blocked(rows_low, low_cols, cols_weight)
     new_diff = VAR_DIFF * apply_blocked(rows_diff, cols_high * inv_len_diff[:, None], cols_hprobe)
-    low_block = lax.all_gather(new_low, "grp", axis=1, tiled=True)
+    low_block = unblock(gather_bits(new_low, "grp", grp_size, GRP_BITS), probes_n)
     high_part = jnp.dot(
         low_block, pick_own, precision=lax.Precision.HIGHEST, preferred_element_type=jnp.float32
     )

time: 1470 us -> 220 us (0.15)
  blocking collectives: 1370 us -> 0 us
  waiting for transfers between devices: 0.74 us -> 51.9 us
  matrix products: 73 us -> 117 us
  starting transfers between devices: 0.08 us -> 22 us
  other arithmetic: 2.38 us -> 20.8 us
    all_gather x5 -> x0, blocking collectives: 1350 us -> none  [the longest x1 627 us: per_device(): lax.all_gather(high_probes, ('blk', 'grp'), axis=1, tiled=True)]
    ppermute x0 -> x11, waiting for transfers between devices: none -> 51.9 us  [gather_bits(): other = lax.ppermute(buf, axis, [(i, i ^ mask) for i in range(size)])]
    dot_general x24, matrix products: 40.2 us -> 69.3 us  [matern(): inner = jnp.einsum('fr,fc->rc', rows, cols, precision=lax.Precision.HIGHEST)]
    ppermute x0 -> x11, starting transfers between devices: none -> 22 us  [gather_bits(): other = lax.ppermute(buf, axis, [(i, i ^ mask) for i in range(size)])]
  transfers between devices with their start and end apart: 2 -> 11, of which waited for: 0 -> 10; matrix products, arithmetic and copies ran while one was open for 1% -> 9% of each run, Pallas kernels for 0% -> 0%
where the time goes in v1:
time: 220 us; the launch traced here: 217 us
  matrix products  117 us (53%)
  waiting for transfers between devices  51.9 us (24%)
  starting transfers between devices  22 us (10%)
  other arithmetic  20.8 us (9%)
  local copies, waits for them, and re-layouts  4 us (2%)
    dot_general x24, matrix products, matern(): inner = jnp.einsum('fr,fc->rc', rows, cols, precision=lax.Precision.HIGHEST)  69.3 us
    ppermute x11, waiting for transfers between devices, gather_bits(): other = lax.ppermute(buf, axis, [(i, i ^ mask) for i in range(size)])  51.9 us
    dot_general x24, matrix products, partial_product(): jnp.einsum('pc,rc->pr', weights, tile, precision=lax.Precision.HIGHEST)  44.2 us
    ppermute x11, starting transfers between devices, gather_bits(): other = lax.ppermute(buf, axis, [(i, i ^ mask) for i in range(size)])  22 us
    reduce_sum x24, other arithmetic, matern(): jnp.sum(cols * cols, 0)[None, :]  14 us
  transfers between devices with their start and end apart: 11, of which 10 were waited for; matrix products, arithmetic and copies ran while one was open for 9% of the time, Pallas kernels for 0%

profile of v1, /device:TPU:16, one launch (start us, length us, event | category | flops | bytes accessed | tf_op | source)
XLA Modules:
  0.0 217.4 jit_solution(4410521709907854774)
XLA Ops:
  2.8 3.1 %collective-permute-start = (f32[1,2624]{1,0:T(1,128)S(1)}, f32[1,2624]{1,0:T(1,128)S(1)}, u32[]{:S(2)}, u32[]{:S(2)}) collective-permute-start(f32[1,2624]{1,0:T(1,128)S(1)} %broadcast_in_dim.13), channel_id=1, source_target_pairs={{0,4},{1,5},{2,6},{3,7},{4,0},{5,1},{6,2},{7,3},{8,12},{9,13},{10,... | collective-permute-start | bytes 31496 | tf_op jit(solution)/shard_map/ppermute | solution.py:48
  5.9 2.2 collective-permute-done
  8.1 2.1 collective-permute-start.1
  10.2 3.3 %collective-permute-done.1 = f32[2,2624]{1,0:T(2,128)S(1)} collective-permute-done((f32[2,2624]{1,0:T(2,128)S(1)}, f32[2,2624]{1,0:T(2,128)S(1)}, u32[]{:S(2)}, u32[]{:S(2)}) %collective-permute-start.1) | collective-permute-done | bytes 21024 | tf_op jit(solution)/shard_map/ppermute | solution.py:48
  15.1 2.5 %collective-permute-done.2 = f32[4,2624]{1,0:T(4,128)S(1)} collective-permute-done((f32[4,2624]{1,0:T(4,128)S(1)}, f32[4,2624]{1,0:T(4,128)S(1)}, u32[]{:S(2)}, u32[]{:S(2)}) %collective-permute-start.2) | collective-permute-done | bytes 42016 | tf_op jit(solution)/shard_map/ppermute | solution.py:48
  20.0 7.3 %collective-permute-start.3 = (f32[1,8,3072]{2,1,0:T(8,128)S(1)}, f32[1,8,3072]{2,1,0:T(8,128)S(1)}, u32[]{:S(2)}, u32[]{:S(2)}) collective-permute-start(f32[1,8,3072]{2,1,0:T(8,128)S(1)} %maximum_bitcast_fusion), channel_id=1, source_target_pairs={{0,128},{8,136},{16,144},{24,152},{32,160},{40,168},{48,176},{56,1... | collective-permute-start | bytes 294920 | tf_op jit(solution)/shard_map/ppermute | solution.py:48
  27.2 3.5 %collective-permute-done.3 = f32[1,8,3072]{2,1,0:T(8,128)S(1)} collective-permute-done((f32[1,8,3072]{2,1,0:T(8,128)S(1)}, f32[1,8,3072]{2,1,0:T(8,128)S(1)}, u32[]{:S(2)}, u32[]{:S(2)}) %collective-permute-start.3) | collective-permute-done | bytes 98336 | tf_op jit(solution)/shard_map/ppermute | solution.py:48
  32.1 7.7 %collective-permute-done.4 = f32[2,8,3072]{2,1,0:T(8,128)S(1)} collective-permute-done((f32[2,8,3072]{2,1,0:T(8,128)S(1)}, f32[2,8,3072]{2,1,0:T(8,128)S(1)}, u32[]{:S(2)}, u32[]{:S(2)}) %collective-permute-start.4) | collective-permute-done | bytes 196640 | tf_op jit(solution)/shard_map/ppermute | solution.py:48
  39.9 9.4 %collective-permute-done.5 = f32[4,8,3072]{2,1,0:T(8,128)S(1)} collective-permute-done((f32[4,8,3072]{2,1,0:T(8,128)S(1)}, f32[4,8,3072]{2,1,0:T(8,128)S(1)}, u32[]{:S(2)}, u32[]{:S(2)}) %collective-permute-start.5) | collective-permute-done | bytes 393248 | tf_op jit(solution)/shard_map/ppermute | solution.py:48
  50.8 15.7 %collective-permute-done.6 = f32[8,8,3072]{2,1,0:T(8,128)S(1)} collective-permute-done((f32[8,8,3072]{2,1,0:T(8,128)S(1)}, f32[8,8,3072]{2,1,0:T(8,128)S(1)}, u32[]{:S(2)}, u32[]{:S(2)}) %collective-permute-start.6) | collective-permute-done | bytes 786464 | tf_op jit(solution)/shard_map/ppermute | solution.py:48
  75.2 110.3 %while.26 = (s32[]{:T(128)}, f32[8,128]{1,0:T(8,128)S(1)}, f32[16,8,2048]{2,1,0:T(8,128)}, f32[128]{0:T(128)S(1)}, f32[16,8,2048]{2,1,0:T(8,128)}, /*index=5*/f32[8,128]{1,0:T(8,128)S(1)}, s32[]{:T(128)}, s32[]{:T(128)}) while((s32[]{:T(128)}, f32[8,128]{1,0:T(8,128)S(1)}, f32[16,8,2048]{2,1,0:T(8,128)}, f32[128]{0:T(128)S(1)}, ...), condition=%wide.region_3.4_spmd.clone, body=%wide.region_1.3_spmd.clone.sunk | while | flops 52461568 | bytes 2324067 | solution.py:39
  76.1 3.9 %fusion.75 = f32[128,2048]{0,1:T(8,128)} fusion(f32[8,128]{1,0:T(8,128)S(1)} %get-tuple-element.329, f32[2048]{0:T(1024)S(1)} %fusion.74, f32[128]{0:T(128)S(1)} %get-tuple-element.327, f32[16,8,2048]{2,1,0:T(8,128)} %get-tuple-element.328, s32[]{:T(128)} %get-tuple-element.316), kind=kOutput, calls=%fused_computation.4.clone.1 | convolution fusion | flops 26214400 | bytes 1127424 | tf_op jit(solution)/shard_map/while/body/eval_jaxpr/fr,fc->rc/dot_general | solution.py:17
  80.0 2.1 convolution_add_fusion.4
  83.0 3.9 %fusion.75 = f32[128,2048]{0,1:T(8,128)} fusion(f32[8,128]{1,0:T(8,128)S(1)} %get-tuple-element.329, f32[2048]{0:T(1024)S(1)} %fusion.74, f32[128]{0:T(128)S(1)} %get-tuple-element.327, f32[16,8,2048]{2,1,0:T(8,128)} %get-tuple-element.328, s32[]{:T(128)} %get-tuple-element.316), kind=kOutput, calls=%fused_computation.4.clone.1 | convolution fusion | flops 26214400 | bytes 1127424 | tf_op jit(solution)/shard_map/while/body/eval_jaxpr/fr,fc->rc/dot_general | solution.py:17
  89.9 3.9 %fusion.75 = f32[128,2048]{0,1:T(8,128)} fusion(f32[8,128]{1,0:T(8,128)S(1)} %get-tuple-element.329, f32[2048]{0:T(1024)S(1)} %fusion.74, f32[128]{0:T(128)S(1)} %get-tuple-element.327, f32[16,8,2048]{2,1,0:T(8,128)} %get-tuple-element.328, s32[]{:T(128)} %get-tuple-element.316), kind=kOutput, calls=%fused_computation.4.clone.1 | convolution fusion | flops 26214400 | bytes 1127424 | tf_op jit(solution)/shard_map/while/body/eval_jaxpr/fr,fc->rc/dot_general | solution.py:17
  96.8 3.9 %fusion.75 = f32[128,2048]{0,1:T(8,128)} fusion(f32[8,128]{1,0:T(8,128)S(1)} %get-tuple-element.329, f32[2048]{0:T(1024)S(1)} %fusion.74, f32[128]{0:T(128)S(1)} %get-tuple-element.327, f32[16,8,2048]{2,1,0:T(8,128)} %get-tuple-element.328, s32[]{:T(128)} %get-tuple-element.316), kind=kOutput, calls=%fused_computation.4.clone.1 | convolution fusion | flops 26214400 | bytes 1127424 | tf_op jit(solution)/shard_map/while/body/eval_jaxpr/fr,fc->rc/dot_general | solution.py:17
  103.7 3.9 %fusion.75 = f32[128,2048]{0,1:T(8,128)} fusion(f32[8,128]{1,0:T(8,128)S(1)} %get-tuple-element.329, f32[2048]{0:T(1024)S(1)} %fusion.74, f32[128]{0:T(128)S(1)} %get-tuple-element.327, f32[16,8,2048]{2,1,0:T(8,128)} %get-tuple-element.328, s32[]{:T(128)} %get-tuple-element.316), kind=kOutput, calls=%fused_computation.4.clone.1 | convolution fusion | flops 26214400 | bytes 1127424 | tf_op jit(solution)/shard_map/while/body/eval_jaxpr/fr,fc->rc/dot_general | solution.py:17
  110.6 3.9 %fusion.75 = f32[128,2048]{0,1:T(8,128)} fusion(f32[8,128]{1,0:T(8,128)S(1)} %get-tuple-element.329, f32[2048]{0:T(1024)S(1)} %fusion.74, f32[128]{0:T(128)S(1)} %get-tuple-element.327, f32[16,8,2048]{2,1,0:T(8,128)} %get-tuple-element.328, s32[]{:T(128)} %get-tuple-element.316), kind=kOutput, calls=%fused_computation.4.clone.1 | convolution fusion | flops 26214400 | bytes 1127424 | tf_op jit(solution)/shard_map/while/body/eval_jaxpr/fr,fc->rc/dot_general | solution.py:17
  114.5 2.1 convolution_add_fusion.4
  117.5 3.9 %fusion.75 = f32[128,2048]{0,1:T(8,128)} fusion(f32[8,128]{1,0:T(8,128)S(1)} %get-tuple-element.329, f32[2048]{0:T(1024)S(1)} %fusion.74, f32[128]{0:T(128)S(1)} %get-tuple-element.327, f32[16,8,2048]{2,1,0:T(8,128)} %get-tuple-element.328, s32[]{:T(128)} %get-tuple-element.316), kind=kOutput, calls=%fused_computation.4.clone.1 | convolution fusion | flops 26214400 | bytes 1127424 | tf_op jit(solution)/shard_map/while/body/eval_jaxpr/fr,fc->rc/dot_general | solution.py:17
  124.4 3.9 %fusion.75 = f32[128,2048]{0,1:T(8,128)} fusion(f32[8,128]{1,0:T(8,128)S(1)} %get-tuple-element.329, f32[2048]{0:T(1024)S(1)} %fusion.74, f32[128]{0:T(128)S(1)} %get-tuple-element.327, f32[16,8,2048]{2,1,0:T(8,128)} %get-tuple-element.328, s32[]{:T(128)} %get-tuple-element.316), kind=kOutput, calls=%fused_computation.4.clone.1 | convolution fusion | flops 26214400 | bytes 1127424 | tf_op jit(solution)/shard_map/while/body/eval_jaxpr/fr,fc->rc/dot_general | solution.py:17
  131.3 3.9 %fusion.75 = f32[128,2048]{0,1:T(8,128)} fusion(f32[8,128]{1,0:T(8,128)S(1)} %get-tuple-element.329, f32[2048]{0:T(1024)S(1)} %fusion.74, f32[128]{0:T(128)S(1)} %get-tuple-element.327, f32[16,8,2048]{2,1,0:T(8,128)} %get-tuple-element.328, s32[]{:T(128)} %get-tuple-element.316), kind=kOutput, calls=%fused_computation.4.clone.1 | convolution fusion | flops 26214400 | bytes 1127424 | tf_op jit(solution)/shard_map/while/body/eval_jaxpr/fr,fc->rc/dot_general | solution.py:17
  138.2 3.9 %fusion.75 = f32[128,2048]{0,1:T(8,128)} fusion(f32[8,128]{1,0:T(8,128)S(1)} %get-tuple-element.329, f32[2048]{0:T(1024)S(1)} %fusion.74, f32[128]{0:T(128)S(1)} %get-tuple-element.327, f32[16,8,2048]{2,1,0:T(8,128)} %get-tuple-element.328, s32[]{:T(128)} %get-tuple-element.316), kind=kOutput, calls=%fused_computation.4.clone.1 | convolution fusion | flops 26214400 | bytes 1127424 | tf_op jit(solution)/shard_map/while/body/eval_jaxpr/fr,fc->rc/dot_general | solution.py:17
  145.1 3.9 %fusion.75 = f32[128,2048]{0,1:T(8,128)} fusion(f32[8,128]{1,0:T(8,128)S(1)} %get-tuple-element.329, f32[2048]{0:T(1024)S(1)} %fusion.74, f32[128]{0:T(128)S(1)} %get-tuple-element.327, f32[16,8,2048]{2,1,0:T(8,128)} %get-tuple-element.328, s32[]{:T(128)} %get-tuple-element.316), kind=kOutput, calls=%fused_computation.4.clone.1 | convolution fusion | flops 26214400 | bytes 1127424 | tf_op jit(solution)/shard_map/while/body/eval_jaxpr/fr,fc->rc/dot_general | solution.py:17
  151.9 3.9 %fusion.75 = f32[128,2048]{0,1:T(8,128)} fusion(f32[8,128]{1,0:T(8,128)S(1)} %get-tuple-element.329, f32[2048]{0:T(1024)S(1)} %fusion.74, f32[128]{0:T(128)S(1)} %get-tuple-element.327, f32[16,8,2048]{2,1,0:T(8,128)} %get-tuple-element.328, s32[]{:T(128)} %get-tuple-element.316), kind=kOutput, calls=%fused_computation.4.clone.1 | convolution fusion | flops 26214400 | bytes 1127424 | tf_op jit(solution)/shard_map/while/body/eval_jaxpr/fr,fc->rc/dot_general | solution.py:17
  158.8 3.9 %fusion.75 = f32[128,2048]{0,1:T(8,128)} fusion(f32[8,128]{1,0:T(8,128)S(1)} %get-tuple-element.329, f32[2048]{0:T(1024)S(1)} %fusion.74, f32[128]{0:T(128)S(1)} %get-tuple-element.327, f32[16,8,2048]{2,1,0:T(8,128)} %get-tuple-element.328, s32[]{:T(128)} %get-tuple-element.316), kind=kOutput, calls=%fused_computation.4.clone.1 | convolution fusion | flops 26214400 | bytes 1127424 | tf_op jit(solution)/shard_map/while/body/eval_jaxpr/fr,fc->rc/dot_general | solution.py:17
  165.7 3.9 %fusion.75 = f32[128,2048]{0,1:T(8,128)} fusion(f32[8,128]{1,0:T(8,128)S(1)} %get-tuple-element.329, f32[2048]{0:T(1024)S(1)} %fusion.74, f32[128]{0:T(128)S(1)} %get-tuple-element.327, f32[16,8,2048]{2,1,0:T(8,128)} %get-tuple-element.328, s32[]{:T(128)} %get-tuple-element.316), kind=kOutput, calls=%fused_computation.4.clone.1 | convolution fusion | flops 26214400 | bytes 1127424 | tf_op jit(solution)/shard_map/while/body/eval_jaxpr/fr,fc->rc/dot_general | solution.py:17
  172.6 3.9 %fusion.75 = f32[128,2048]{0,1:T(8,128)} fusion(f32[8,128]{1,0:T(8,128)S(1)} %get-tuple-element.329, f32[2048]{0:T(1024)S(1)} %fusion.74, f32[128]{0:T(128)S(1)} %get-tuple-element.327, f32[16,8,2048]{2,1,0:T(8,128)} %get-tuple-element.328, s32[]{:T(128)} %get-tuple-element.316), kind=kOutput, calls=%fused_computation.4.clone.1 | convolution fusion | flops 26214400 | bytes 1127424 | tf_op jit(solution)/shard_map/while/body/eval_jaxpr/fr,fc->rc/dot_general | solution.py:17
  179.5 3.9 %fusion.75 = f32[128,2048]{0,1:T(8,128)} fusion(f32[8,128]{1,0:T(8,128)S(1)} %get-tuple-element.329, f32[2048]{0:T(1024)S(1)} %fusion.74, f32[128]{0:T(128)S(1)} %get-tuple-element.327, f32[16,8,2048]{2,1,0:T(8,128)} %get-tuple-element.328, s32[]{:T(128)} %get-tuple-element.316), kind=kOutput, calls=%fused_computation.4.clone.1 | convolution fusion | flops 26214400 | bytes 1127424 | tf_op jit(solution)/shard_map/while/body/eval_jaxpr/fr,fc->rc/dot_general | solution.py:17
  185.6 3.1 %collective-permute-start.8 = (f32[1,8,128]{2,1,0:T(8,128)S(1)}, f32[1,8,128]{2,1,0:T(8,128)S(1)}, u32[]{:S(2)}, u32[]{:S(2)}) collective-permute-start(f32[1,8,128]{2,1,0:T(8,128)S(1)} %bitcast.132), channel_id=1, source_target_pairs={{0,4},{1,5},{2,6},{3,7},{4,0},{5,1},{6,2},{7,3},{8,12},{9,13},{10,... | collective-permute-start | bytes 12296 | tf_op jit(solution)/shard_map/ppermute | solution.py:48
  191.2 4.7 %collective-permute-done.9 = f32[2,8,128]{2,1,0:T(8,128)S(1)} collective-permute-done((f32[2,8,128]{2,1,0:T(8,128)S(1)}, f32[2,8,128]{2,1,0:T(8,128)S(1)}, u32[]{:S(2)}, u32[]{:S(2)}) %collective-permute-start.9) | collective-permute-done | bytes 8224 | tf_op jit(solution)/shard_map/ppermute | solution.py:48
  197.5 17.9 %while.27 = (s32[]{:T(128)}, f32[8,64]{1,0:T(8,128)S(1)}, f32[8,8,2048]{2,1,0:T(8,128)}, f32[64]{0:T(128)S(1)}, f32[8,8,2048]{2,1,0:T(8,128)S(1)}, /*index=5*/f32[8,64]{1,0:T(8,128)S(1)}, s32[]{:T(128)}, s32[]{:T(128)}) while((s32[]{:T(128)}, f32[8,64]{1,0:T(8,128)S(1)}, f32[8,8,2048]{2,1,0:T(8,128)}, f32[64]{0:T(128)S(1)}, ...), condition=%wide.region_7.8_spmd.clone, body=%wide.region_5.7_spmd.clone.sunk | while | flops 26246148 | bytes 1270887 | solution.py:39
  (124 shorter events, 84.0 us)
Async XLA Ops:
  2.8 5.3 %collective-permute-start = (f32[1,2624]{1,0:T(1,128)S(1)}, f32[1,2624]{1,0:T(1,128)S(1)}, u32[]{:S(2)}, u32[]{:S(2)}) collective-permute-start(f32[1,2624]{1,0:T(1,128)S(1)} %broadcast_in_dim.13), channel_id=1, source_target_pairs={{0,4},{1,5},{2,6},{3,7},{4,0},{5,1},{6,2},{7,3},{8,12},{9,13},{10,... | collective-permute-start | bytes 31496 | tf_op jit(solution)/shard_map/ppermute | solution.py:48
  8.1 5.4 %collective-permute-start.1 = (f32[2,2624]{1,0:T(2,128)S(1)}, f32[2,2624]{1,0:T(2,128)S(1)}, u32[]{:S(2)}, u32[]{:S(2)}) collective-permute-start(f32[2,2624]{1,0:T(2,128)S(1)} %pad_maximum_fusion.8), channel_id=1, source_target_pairs={{0,1},{1,0},{2,3},{3,2},{4,5},{5,4},{6,7},{7,6},{8,9},{9,8},{10,11... | collective-permute-start | bytes 62984 | tf_op jit(solution)/shard_map/ppermute | solution.py:48
  13.5 4.1 %collective-permute-start.2 = (f32[4,2624]{1,0:T(4,128)S(1)}, f32[4,2624]{1,0:T(4,128)S(1)}, u32[]{:S(2)}, u32[]{:S(2)}) collective-permute-start(f32[4,2624]{1,0:T(4,128)S(1)} %pad_maximum_fusion.6), channel_id=1, source_target_pairs={{0,2},{1,3},{2,0},{3,1},{4,6},{5,7},{6,4},{7,5},{8,10},{9,11},{10,... | collective-permute-start | bytes 125960 | tf_op jit(solution)/shard_map/ppermute | solution.py:48
  20.0 10.8 %collective-permute-start.3 = (f32[1,8,3072]{2,1,0:T(8,128)S(1)}, f32[1,8,3072]{2,1,0:T(8,128)S(1)}, u32[]{:S(2)}, u32[]{:S(2)}) collective-permute-start(f32[1,8,3072]{2,1,0:T(8,128)S(1)} %maximum_bitcast_fusion), channel_id=1, source_target_pairs={{0,128},{8,136},{16,144},{24,152},{32,160},{40,168},{48,176},{56,1... | collective-permute-start | bytes 294920 | tf_op jit(solution)/shard_map/ppermute | solution.py:48
  30.8 9.0 %collective-permute-start.4 = (f32[2,8,3072]{2,1,0:T(8,128)S(1)}, f32[2,8,3072]{2,1,0:T(8,128)S(1)}, u32[]{:S(2)}, u32[]{:S(2)}) collective-permute-start(f32[2,8,3072]{2,1,0:T(8,128)S(1)} %pad_maximum_fusion.4), channel_id=1, source_target_pairs={{0,64},{8,72},{16,80},{24,88},{32,96},{40,104},{48,112},{56,120},{... | collective-permute-start | bytes 589832 | tf_op jit(solution)/shard_map/ppermute | solution.py:48
  39.8 9.5 %collective-permute-start.5 = (f32[4,8,3072]{2,1,0:T(8,128)S(1)}, f32[4,8,3072]{2,1,0:T(8,128)S(1)}, u32[]{:S(2)}, u32[]{:S(2)}) collective-permute-start(f32[4,8,3072]{2,1,0:T(8,128)S(1)} %pad_maximum_fusion.3), channel_id=1, source_target_pairs={{0,32},{8,40},{16,48},{24,56},{32,0},{40,8},{48,16},{56,24},{64,96... | collective-permute-start | bytes 1179656 | tf_op jit(solution)/shard_map/ppermute | solution.py:48
  49.5 17.1 %collective-permute-start.6 = (f32[8,8,3072]{2,1,0:T(8,128)S(1)}, f32[8,8,3072]{2,1,0:T(8,128)S(1)}, u32[]{:S(2)}, u32[]{:S(2)}) collective-permute-start(f32[8,8,3072]{2,1,0:T(8,128)S(1)} %pad_maximum_fusion.2), channel_id=1, source_target_pairs={{0,16},{8,24},{16,0},{24,8},{32,48},{40,56},{48,32},{56,40},{64,80... | collective-permute-start | bytes 2359304 | tf_op jit(solution)/shard_map/ppermute | solution.py:48
  66.7 0.7 copy-start
  66.7 0.7 copy-start.2
  66.7 0.8 copy-start.3
  66.9 3.6 %collective-permute-start.7 = (f32[16,8,3072]{2,1,0:T(8,128)S(1)}, f32[16,8,3072]{2,1,0:T(8,128)}, u32[]{:S(2)}, u32[]{:S(2)}) collective-permute-start(f32[16,8,3072]{2,1,0:T(8,128)S(1)} %pad_maximum_fusion.1), channel_id=1, source_target_pairs={{0,8},{8,0},{16,24},{24,16},{32,40},{40,32},{48,56},{56,48},{64,72... | collective-permute-start | bytes 4718600 | tf_op jit(solution)/shard_map/ppermute | solution.py:48
  185.6 5.7 %copy-start.1 = (f32[8,128]{1,0:T(8,128)}, f32[8,128]{1,0:T(8,128)S(1)}, u32[]{:S(2)}) copy-start(f32[8,128]{1,0:T(8,128)S(1)} %get-tuple-element.132) | copy-start | bytes 12292
  185.6 5.2 %collective-permute-start.8 = (f32[1,8,128]{2,1,0:T(8,128)S(1)}, f32[1,8,128]{2,1,0:T(8,128)S(1)}, u32[]{:S(2)}, u32[]{:S(2)}) collective-permute-start(f32[1,8,128]{2,1,0:T(8,128)S(1)} %bitcast.132), channel_id=1, source_target_pairs={{0,4},{1,5},{2,6},{3,7},{4,0},{5,1},{6,2},{7,3},{8,12},{9,13},{10,... | collective-permute-start | bytes 12296 | tf_op jit(solution)/shard_map/ppermute | solution.py:48
  190.8 5.2 %collective-permute-start.9 = (f32[2,8,128]{2,1,0:T(8,128)S(1)}, f32[2,8,128]{2,1,0:T(8,128)S(1)}, u32[]{:S(2)}, u32[]{:S(2)}) collective-permute-start(f32[2,8,128]{2,1,0:T(8,128)S(1)} %pad_maximum_fusion.11), channel_id=1, source_target_pairs={{0,1},{1,0},{2,3},{3,2},{4,5},{5,4},{6,7},{7,6},{8,9},{9,8},{10,11... | collective-permute-start | bytes 24584 | tf_op jit(solution)/shard_map/ppermute | solution.py:48
  195.9 19.5 %collective-permute-start.10 = (f32[4,8,128]{2,1,0:T(8,128)S(1)}, f32[4,8,128]{2,1,0:T(8,128)S(1)}, u32[]{:S(2)}, u32[]{:S(2)}) collective-permute-start(f32[4,8,128]{2,1,0:T(8,128)S(1)} %pad_maximum_fusion.9), channel_id=1, source_target_pairs={{0,2},{1,3},{2,0},{3,1},{4,6},{5,7},{6,4},{7,5},{8,10},{9,11},{10,... | collective-permute-start | bytes 49160 | tf_op jit(solution)/shard_map/ppermute | solution.py:48

commit v2 on v1

--- a/solution.py
+++ b/solution.py
@@ -3,6 +3,8 @@
 import jax
 import jax.numpy as jnp
 from jax import lax
+from jax.experimental import pallas as pl
+from jax.experimental.pallas import tpu as pltpu
 from jax.sharding import PartitionSpec as P
 
 RHO = 0.9
@@ -38,6 +40,57 @@
     start = jnp.zeros((weights.shape[0], rows.shape[1]), jnp.float32)
     total, _ = lax.scan(one_block, start, (cols_split, weights_split))
     return total
+
+
+COL_TILE = 4096
+COL_SUB = 512
+
+
+def _matvec_kernel(rows_ref, cols_ref, w_ref, out_ref):
+    @pl.when(pl.program_id(0) == 0)
+    def _init():
+        out_ref[...] = jnp.zeros(out_ref.shape, jnp.float32)
+
+    rows = rows_ref[...]
+    rn = jnp.sum(rows * rows, axis=1, keepdims=True)
+
+    def body(i, acc):
+        start = pl.multiple_of(i * COL_SUB, COL_SUB)
+        cols = cols_ref[:, pl.ds(start, COL_SUB)]
+        w = w_ref[:, pl.ds(start, COL_SUB)]
+        inner = jnp.dot(rows, cols, precision=lax.Precision.HIGHEST, preferred_element_type=jnp.float32)
+        cn = jnp.sum(cols * cols, axis=0, keepdims=True)
+        square = rn + cn - 2.0 * inner
+        dist = jnp.sqrt(jnp.maximum(square, 0.0))
+        tile = (1.0 + SQRT_THREE * dist) * jnp.exp(-SQRT_THREE * dist)
+        return acc + lax.dot_general(
+            w, tile, (((1,), (1,)), ((), ())),
+            precision=lax.Precision.HIGHEST, preferred_element_type=jnp.float32,
+        )
+
+    steps = cols_ref.shape[1] // COL_SUB
+    acc = lax.fori_loop(0, steps, body, jnp.zeros(out_ref.shape, jnp.float32))
+    out_ref[...] += acc
+
+
+def apply_fused(rows, cols, weights, interpret=False):
+    feats, count = cols.shape
+    nrows = rows.shape[1]
+    probes = weights.shape[0]
+    tile = min(COL_TILE, count)
+    return pl.pallas_call(
+        _matvec_kernel,
+        grid=(count // tile,),
+        in_specs=[
+            pl.BlockSpec((nrows, feats), lambda j: (0, 0)),
+            pl.BlockSpec((feats, tile), lambda j: (0, j)),
+            pl.BlockSpec((probes, tile), lambda j: (0, j)),
+        ],
+        out_specs=pl.BlockSpec((probes, nrows), lambda j: (0, 0)),
+        out_shape=jax.ShapeDtypeStruct((probes, nrows), jnp.float32),
+        compiler_params=pltpu.CompilerParams(dimension_semantics=("arbitrary",)),
+        interpret=interpret,
+    )(rows.T, cols, weights)
 
 
 def gather_bits(x, axis, size, bits):
@@ -117,8 +170,8 @@
     rows_low = low_sites * inv_len_low[:, None]
     rows_diff = high_feats * inv_len_diff[:, None]
     low_cols = cols_feat * inv_len_low[:, None]
-    new_low = apply_blocked(rows_low, low_cols, cols_weight)
-    new_diff = VAR_DIFF * apply_blocked(rows_diff, cols_high * inv_len_diff[:, None], cols_hprobe)
+    new_low = apply_fused(rows_low, low_cols, cols_weight)
+    new_diff = VAR_DIFF * apply_fused(rows_diff, cols_high * inv_len_diff[:, None], cols_hprobe)
     low_block = unblock(gather_bits(new_low, "grp", grp_size, GRP_BITS), probes_n)
     high_part = jnp.dot(
         low_block, pick_own, precision=lax.Precision.HIGHEST, preferred_element_type=jnp.float32

time: 220 us -> 157 us (0.71); the launches traced: 217 us -> 157 us
  matrix products: 117 us -> 3.65 us
  Pallas kernels: 0 us -> 66.5 us
  other arithmetic: 20.8 us -> 8.6 us
    dot_general x48 -> x0, matrix products: 113 us -> none  [the longest x24 69.3 us: matern(): inner = jnp.einsum('fr,fc->rc', rows, cols, precision=lax.Precision.HIGHEST)]
    pallas_call x0 -> x2, Pallas kernels: none -> 66.5 us  [apply_fused(): pl.pallas_call(_matvec_kernel, grid=(count // tile,), in_specs=[pl.BlockS...]
    reduce_sum x26 -> x0, other arithmetic: 14.2 us -> none  [the longest x24 14 us: matern(): jnp.sum(cols * cols, 0)[None, :]]
  transfers between devices with their start and end apart: 11 -> 11, of which waited for: 10 -> 10; matrix products, arithmetic and copies ran while one was open for 9% -> 3% of each run, Pallas kernels for 0% -> 11%
where the time goes in v2:
time: 157 us
  Pallas kernels  66.5 us (42%)
  waiting for transfers between devices  50.8 us (32%)
  starting transfers between devices  21.9 us (14%)
  other arithmetic  8.6 us (5%)
  local copies, waits for them, and re-layouts  4.82 us (3%)
  matrix products  3.65 us (2%)
    pallas_call x2, Pallas kernels, apply_fused(): pl.pallas_call(_matvec_kernel, grid=(count // tile,), in_specs=[pl.BlockS...  66.5 us
    ppermute x11, waiting for transfers between devices, gather_bits(): other = lax.ppermute(buf, axis, [(i, i ^ mask) for i in range(size)])  50.8 us
    ppermute x11, starting transfers between devices, gather_bits(): other = lax.ppermute(buf, axis, [(i, i ^ mask) for i in range(size)])  21.9 us
  transfers between devices with their start and end apart: 11, of which 10 were waited for; matrix products, arithmetic and copies ran while one was open for 3% of the time, Pallas kernels for 11%

profile of v2, /device:TPU:16, one launch (start us, length us, event | category | flops | bytes accessed | tf_op | source)
XLA Modules:
  0.0 157.2 jit_solution(2588599480685459297)
XLA Ops:
  0.6 0.8 reshape.78
  2.0 0.7 pad_maximum_fusion.10
  2.8 3.1 %collective-permute-start = (f32[1,2624]{1,0:T(1,128)S(1)}, f32[1,2624]{1,0:T(1,128)S(1)}, u32[]{:S(2)}, u32[]{:S(2)}) collective-permute-start(f32[1,2624]{1,0:T(1,128)S(1)} %broadcast_in_dim.6), channel_id=1, source_target_pairs={{0,4},{1,5},{2,6},{3,7},{4,0},{5,1},{6,2},{7,3},{8,12},{9,13},{10,... | collective-permute-start | bytes 31496 | tf_op jit(solution)/shard_map/ppermute | solution.py:101
  5.9 2.2 %collective-permute-done = f32[1,2624]{1,0:T(1,128)S(1)} collective-permute-done((f32[1,2624]{1,0:T(1,128)S(1)}, f32[1,2624]{1,0:T(1,128)S(1)}, u32[]{:S(2)}, u32[]{:S(2)}) %collective-permute-start) | collective-permute-done | bytes 10528 | tf_op jit(solution)/shard_map/ppermute | solution.py:101
  8.1 2.1 %collective-permute-start.1 = (f32[2,2624]{1,0:T(2,128)S(1)}, f32[2,2624]{1,0:T(2,128)S(1)}, u32[]{:S(2)}, u32[]{:S(2)}) collective-permute-start(f32[2,2624]{1,0:T(2,128)S(1)} %pad_maximum_fusion.8), channel_id=1, source_target_pairs={{0,1},{1,0},{2,3},{3,2},{4,5},{5,4},{6,7},{7,6},{8,9},{9,8},{10,11... | collective-permute-start | bytes 62984 | tf_op jit(solution)/shard_map/ppermute | solution.py:101
  10.2 3.3 %collective-permute-done.1 = f32[2,2624]{1,0:T(2,128)S(1)} collective-permute-done((f32[2,2624]{1,0:T(2,128)S(1)}, f32[2,2624]{1,0:T(2,128)S(1)}, u32[]{:S(2)}, u32[]{:S(2)}) %collective-permute-start.1) | collective-permute-done | bytes 21024 | tf_op jit(solution)/shard_map/ppermute | solution.py:101
  13.5 1.6 %collective-permute-start.2 = (f32[4,2624]{1,0:T(4,128)S(1)}, f32[4,2624]{1,0:T(4,128)S(1)}, u32[]{:S(2)}, u32[]{:S(2)}) collective-permute-start(f32[4,2624]{1,0:T(4,128)S(1)} %pad_maximum_fusion.6), channel_id=1, source_target_pairs={{0,2},{1,3},{2,0},{3,1},{4,6},{5,7},{6,4},{7,5},{8,10},{9,11},{10,... | collective-permute-start | bytes 125960 | tf_op jit(solution)/shard_map/ppermute | solution.py:101
  15.1 2.5 %collective-permute-done.2 = f32[4,2624]{1,0:T(4,128)S(1)} collective-permute-done((f32[4,2624]{1,0:T(4,128)S(1)}, f32[4,2624]{1,0:T(4,128)S(1)}, u32[]{:S(2)}, u32[]{:S(2)}) %collective-permute-start.2) | collective-permute-done | bytes 42016 | tf_op jit(solution)/shard_map/ppermute | solution.py:101
  18.2 0.7 fusion.2
  18.9 1.0 fusion
  20.0 7.3 %collective-permute-start.3 = (f32[1,8,3072]{2,1,0:T(8,128)S(1)}, f32[1,8,3072]{2,1,0:T(8,128)S(1)}, u32[]{:S(2)}, u32[]{:S(2)}) collective-permute-start(f32[1,8,3072]{2,1,0:T(8,128)S(1)} %maximum_bitcast_fusion), channel_id=1, source_target_pairs={{0,128},{8,136},{16,144},{24,152},{32,160},{40,168},{48,176},{56,1... | collective-permute-start | bytes 294920 | tf_op jit(solution)/shard_map/ppermute | solution.py:101
  27.2 3.5 %collective-permute-done.3 = f32[1,8,3072]{2,1,0:T(8,128)S(1)} collective-permute-done((f32[1,8,3072]{2,1,0:T(8,128)S(1)}, f32[1,8,3072]{2,1,0:T(8,128)S(1)}, u32[]{:S(2)}, u32[]{:S(2)}) %collective-permute-start.3) | collective-permute-done | bytes 98336 | tf_op jit(solution)/shard_map/ppermute | solution.py:101
  30.8 1.3 collective-permute-start.4
  32.1 7.7 %collective-permute-done.4 = f32[2,8,3072]{2,1,0:T(8,128)S(1)} collective-permute-done((f32[2,8,3072]{2,1,0:T(8,128)S(1)}, f32[2,8,3072]{2,1,0:T(8,128)S(1)}, u32[]{:S(2)}, u32[]{:S(2)}) %collective-permute-start.4) | collective-permute-done | bytes 196640 | tf_op jit(solution)/shard_map/ppermute | solution.py:101
  39.9 9.4 %collective-permute-done.5 = f32[4,8,3072]{2,1,0:T(8,128)S(1)} collective-permute-done((f32[4,8,3072]{2,1,0:T(8,128)S(1)}, f32[4,8,3072]{2,1,0:T(8,128)S(1)}, u32[]{:S(2)}, u32[]{:S(2)}) %collective-permute-start.5) | collective-permute-done | bytes 393248 | tf_op jit(solution)/shard_map/ppermute | solution.py:101
  49.5 1.4 collective-permute-start.6
  50.8 15.7 %collective-permute-done.6 = f32[8,8,3072]{2,1,0:T(8,128)S(1)} collective-permute-done((f32[8,8,3072]{2,1,0:T(8,128)S(1)}, f32[8,8,3072]{2,1,0:T(8,128)S(1)}, u32[]{:S(2)}, u32[]{:S(2)}) %collective-permute-start.6) | collective-permute-done | bytes 786464 | tf_op jit(solution)/shard_map/ppermute | solution.py:101
  67.4 0.7 copy.29
  68.3 1.2 iota_compare_fusion
  69.5 1.0 collective-permute-done.7
  70.5 1.7 %broadcast_select_fusion.1 = (f32[16,8,3072]{2,1,0:T(8,128)S(1)}, f32[16,8,3072]{2,1,0:T(8,128)S(1)}) fusion(f32[16,8,3072]{2,1,0:T(8,128)} %collective-permute-done.7, pred[]{:T(512)S(6)} %eq.40, f32[8,8,3072]{2,1,0:T(8,128)S(1)} %get-tuple-element.9, f32[8,8,3072]{2,1,0:T(8,128)S(1)} %get-tuple-element.8), kind=kLoop, calls=%fused_computation.12 | loop fusion | flops 1179648 | bytes 6291457 | tf_op jit(solution)/shard_map/jit(_where)/select_n | solution.py:103
  72.7 1.2 fusion.9
  73.9 1.1 broadcast_multiply_fusion.cols_ref
  75.0 48.9 %shard_map.77 = f32[8,128]{1,0:T(8,128)} custom-call(f32[128,8]{1,0:T(8,128)} %bitcast.66, f32[8,32768]{1,0:T(8,128)} %broadcast_multiply_fusion.cols_ref, f32[8,32768]{1,0:T(8,128)} %bitcast.60), custom_call_target="tpu_custom_call" | custom-call | tf_op jit(solution)/shard_map/pallas_call | solution.py:81
  123.9 3.0 %collective-permute-start.8 = (f32[1,8,128]{2,1,0:T(8,128)}, f32[1,8,128]{2,1,0:T(8,128)S(1)}, u32[]{:S(2)}, u32[]{:S(2)}) collective-permute-start(f32[1,8,128]{2,1,0:T(8,128)} %bitcast.70), channel_id=1, source_target_pairs={{0,4},{1,5},{2,6},{3,7},{4,0},{5,1},{6,2},{7,3},{8,12},{9,13},{10,... | collective-permute-start | bytes 12296 | tf_op jit(solution)/shard_map/ppermute | solution.py:101
  127.5 1.7 %collective-permute-done.8 = f32[1,8,128]{2,1,0:T(8,128)S(1)} collective-permute-done((f32[1,8,128]{2,1,0:T(8,128)}, f32[1,8,128]{2,1,0:T(8,128)S(1)}, u32[]{:S(2)}, u32[]{:S(2)}) %collective-permute-start.8) | collective-permute-done | bytes 4128 | tf_op jit(solution)/shard_map/ppermute | solution.py:101
  130.3 0.9 fusion.8
  131.1 3.9 %collective-permute-done.9 = f32[2,8,128]{2,1,0:T(8,128)S(1)} collective-permute-done((f32[2,8,128]{2,1,0:T(8,128)S(1)}, f32[2,8,128]{2,1,0:T(8,128)S(1)}, u32[]{:S(2)}, u32[]{:S(2)}) %collective-permute-start.9) | collective-permute-done | bytes 8224 | tf_op jit(solution)/shard_map/ppermute | solution.py:101
  135.1 1.6 collective-permute-start.10
  136.7 0.9 broadcast_multiply_fusion.1.cols_ref
  137.6 17.6 %shard_map.78 = f32[8,64]{1,0:T(8,128)} custom-call(f32[64,8]{1,0:T(8,128)} %multiply_bitcast_fusion.rows_ref, f32[8,16384]{1,0:T(8,128)} %broadcast_multiply_fusion.1.cols_ref, f32[8,16384]{1,0:T(8,128)} %bitcast.61), custom_call_target="tpu_custom_call" | custom-call | tf_op jit(solution)/shard_map/pallas_call | solution.py:81
  155.3 1.9 %fusion.1 = f32[8,64]{1,0:T(8,128)} fusion(f32[8,64]{1,0:T(8,128)} %shard_map.78, f32[8,1024]{1,0:T(8,128)S(1)} %bitcast.69, pred[1024,512]{1,0:T(32,128)(4,1)} %iota_compare_fusion, s32[]{:T(128)S(6)} %select_n.169), kind=kOutput, calls=%fused_computation.6 | convolution fusion | flops 6292480 | bytes 169988 | tf_op jit(solution)/shard_map/dot_general | solution.py:176
  (51 shorter events, 4.8 us)
Async XLA Ops:
  2.8 5.3 %collective-permute-start = (f32[1,2624]{1,0:T(1,128)S(1)}, f32[1,2624]{1,0:T(1,128)S(1)}, u32[]{:S(2)}, u32[]{:S(2)}) collective-permute-start(f32[1,2624]{1,0:T(1,128)S(1)} %broadcast_in_dim.6), channel_id=1, source_target_pairs={{0,4},{1,5},{2,6},{3,7},{4,0},{5,1},{6,2},{7,3},{8,12},{9,13},{10,... | collective-permute-start | bytes 31496 | tf_op jit(solution)/shard_map/ppermute | solution.py:101
  8.1 5.4 %collective-permute-start.1 = (f32[2,2624]{1,0:T(2,128)S(1)}, f32[2,2624]{1,0:T(2,128)S(1)}, u32[]{:S(2)}, u32[]{:S(2)}) collective-permute-start(f32[2,2624]{1,0:T(2,128)S(1)} %pad_maximum_fusion.8), channel_id=1, source_target_pairs={{0,1},{1,0},{2,3},{3,2},{4,5},{5,4},{6,7},{7,6},{8,9},{9,8},{10,11... | collective-permute-start | bytes 62984 | tf_op jit(solution)/shard_map/ppermute | solution.py:101
  13.5 4.1 %collective-permute-start.2 = (f32[4,2624]{1,0:T(4,128)S(1)}, f32[4,2624]{1,0:T(4,128)S(1)}, u32[]{:S(2)}, u32[]{:S(2)}) collective-permute-start(f32[4,2624]{1,0:T(4,128)S(1)} %pad_maximum_fusion.6), channel_id=1, source_target_pairs={{0,2},{1,3},{2,0},{3,1},{4,6},{5,7},{6,4},{7,5},{8,10},{9,11},{10,... | collective-permute-start | bytes 125960 | tf_op jit(solution)/shard_map/ppermute | solution.py:101
  20.0 10.8 %collective-permute-start.3 = (f32[1,8,3072]{2,1,0:T(8,128)S(1)}, f32[1,8,3072]{2,1,0:T(8,128)S(1)}, u32[]{:S(2)}, u32[]{:S(2)}) collective-permute-start(f32[1,8,3072]{2,1,0:T(8,128)S(1)} %maximum_bitcast_fusion), channel_id=1, source_target_pairs={{0,128},{8,136},{16,144},{24,152},{32,160},{40,168},{48,176},{56,1... | collective-permute-start | bytes 294920 | tf_op jit(solution)/shard_map/ppermute | solution.py:101
  30.8 9.0 %collective-permute-start.4 = (f32[2,8,3072]{2,1,0:T(8,128)S(1)}, f32[2,8,3072]{2,1,0:T(8,128)S(1)}, u32[]{:S(2)}, u32[]{:S(2)}) collective-permute-start(f32[2,8,3072]{2,1,0:T(8,128)S(1)} %pad_maximum_fusion.4), channel_id=1, source_target_pairs={{0,64},{8,72},{16,80},{24,88},{32,96},{40,104},{48,112},{56,120},{... | collective-permute-start | bytes 589832 | tf_op jit(solution)/shard_map/ppermute | solution.py:101
  39.8 9.5 %collective-permute-start.5 = (f32[4,8,3072]{2,1,0:T(8,128)S(1)}, f32[4,8,3072]{2,1,0:T(8,128)S(1)}, u32[]{:S(2)}, u32[]{:S(2)}) collective-permute-start(f32[4,8,3072]{2,1,0:T(8,128)S(1)} %pad_maximum_fusion.3), channel_id=1, source_target_pairs={{0,32},{8,40},{16,48},{24,56},{32,0},{40,8},{48,16},{56,24},{64,96... | collective-permute-start | bytes 1179656 | tf_op jit(solution)/shard_map/ppermute | solution.py:101
  49.5 17.1 %collective-permute-start.6 = (f32[8,8,3072]{2,1,0:T(8,128)S(1)}, f32[8,8,3072]{2,1,0:T(8,128)S(1)}, u32[]{:S(2)}, u32[]{:S(2)}) collective-permute-start(f32[8,8,3072]{2,1,0:T(8,128)S(1)} %pad_maximum_fusion.2), channel_id=1, source_target_pairs={{0,16},{8,24},{16,0},{24,8},{32,48},{40,56},{48,32},{56,40},{64,80... | collective-permute-start | bytes 2359304 | tf_op jit(solution)/shard_map/ppermute | solution.py:101
  66.7 0.7 copy-start
  66.7 0.7 copy-start.2
  66.8 3.6 %collective-permute-start.7 = (f32[16,8,3072]{2,1,0:T(8,128)S(1)}, f32[16,8,3072]{2,1,0:T(8,128)}, u32[]{:S(2)}, u32[]{:S(2)}) collective-permute-start(f32[16,8,3072]{2,1,0:T(8,128)S(1)} %pad_maximum_fusion.1), channel_id=1, source_target_pairs={{0,8},{8,0},{16,24},{24,16},{32,40},{40,32},{48,56},{56,48},{64,72... | collective-permute-start | bytes 4718600 | tf_op jit(solution)/shard_map/ppermute | solution.py:101
  75.0 51.9 %copy-start.1 = (f32[8]{0:T(128)S(1)}, f32[8]{0:T(128)}, u32[]{:S(2)}) copy-start(f32[8]{0:T(128)} %param.11) | copy-start | bytes 100
  123.9 5.3 %collective-permute-start.8 = (f32[1,8,128]{2,1,0:T(8,128)}, f32[1,8,128]{2,1,0:T(8,128)S(1)}, u32[]{:S(2)}, u32[]{:S(2)}) collective-permute-start(f32[1,8,128]{2,1,0:T(8,128)} %bitcast.70), channel_id=1, source_target_pairs={{0,4},{1,5},{2,6},{3,7},{4,0},{5,1},{6,2},{7,3},{8,12},{9,13},{10,... | collective-permute-start | bytes 12296 | tf_op jit(solution)/shard_map/ppermute | solution.py:101
  129.9 5.2 %collective-permute-start.9 = (f32[2,8,128]{2,1,0:T(8,128)S(1)}, f32[2,8,128]{2,1,0:T(8,128)S(1)}, u32[]{:S(2)}, u32[]{:S(2)}) collective-permute-start(f32[2,8,128]{2,1,0:T(8,128)S(1)} %pad_maximum_fusion.11), channel_id=1, source_target_pairs={{0,1},{1,0},{2,3},{3,2},{4,5},{5,4},{6,7},{7,6},{8,9},{9,8},{10,11... | collective-permute-start | bytes 24584 | tf_op jit(solution)/shard_map/ppermute | solution.py:101
  135.1 20.1 %collective-permute-start.10 = (f32[4,8,128]{2,1,0:T(8,128)S(1)}, f32[4,8,128]{2,1,0:T(8,128)S(1)}, u32[]{:S(2)}, u32[]{:S(2)}) collective-permute-start(f32[4,8,128]{2,1,0:T(8,128)S(1)} %pad_maximum_fusion.9), channel_id=1, source_target_pairs={{0,2},{1,3},{2,0},{3,1},{4,6},{5,7},{6,4},{7,5},{8,10},{9,11},{10,... | collective-permute-start | bytes 49160 | tf_op jit(solution)/shard_map/ppermute | solution.py:101
